TPU v7x, 512 devices: a whole 4x4x16 slice. The times are simulated.
512 devices in a mesh: dp: 32 (over z, core), cent: 16 (over y, x).
Axes of the slice: x: 4, y: 4, z: 16, core: 2. Of those that a mesh axis runs over, the one named last changes fastest.
Arguments:
- points: bfloat16 [131072, 1024], P(('dp', 'cent')), may hold values from -22 to 22, as said below
- block_list: int32 [4096, 3], P(('dp', 'cent')), may hold values from 0 to 15, all different within a row; in each aligned block of 8 rows (0 to 7, 8 to 15, ...) at most 2 rows name the same one
- list_count: int32 [4096], P(('dp', 'cent')), may hold values from 1 to 3
- centroids: bfloat16 [16, 1024, 1024], P('cent', 'dp'), may hold values from -14 to 14, as said below
Outputs:
- new_centroids: float32 [16, 1024, 1024], P('cent', 'dp')
Inputs may be any that keep to these rules, and one draw needn't show every extreme that they name: `block_list`: within the rows of one device (aligned blocks of 8 rows) no block id appears more than 2 times, and the ids of one row differ. Only the first list_count[t] entries of row t of block_list are valid. `points`: Real-valued embeddings. Real-valued centroids.
All inputs are finite; a program needn't handle non-finite values.
Results may differ from a plain program's by a relative error of at most 0.0019.
Values may be sent and summed in bfloat16 or wider, within the bound.
No kernel may reach another device: no remote copies, remote signals or barrier semaphores. Data moves between devices by JAX's collectives and lax.ppermute only.
A program may use at most 64 MiB of HBM per device.

v0:
```python
import math
import jax
import jax.numpy as jnp
from jax import lax
from jax.sharding import PartitionSpec as P

score_scale = 2.0
prior_weight = 1.0
empty_norm = 1e30


def combine_norms(peaks, totals, usable):
    keep = usable[..., None]
    highest = jnp.max(jnp.where(keep, peaks, -1e30), axis=-2)
    summed = jnp.sum(jnp.where(keep, totals * jnp.exp(peaks - highest[..., None, :]), 0.0), axis=-2)
    return highest + jnp.log(summed)


def per_device(points, block_list, list_count, centroids):
    owners = lax.axis_size("cent")
    tiles_here, listed = block_list.shape
    width = points.shape[1]
    tile_rows = points.shape[0] // tiles_here
    capacity = (tiles_here * listed + owners - 1) // owners
    slot_rows = capacity * tile_rows
    scale = score_scale / math.sqrt(width)
    usable = jnp.arange(listed, dtype=jnp.int32)[None, :] < list_count[:, None]
    naming = jnp.logical_and(
        block_list[:, :, None] == jnp.arange(owners, dtype=jnp.int32)[None, None, :],
        usable[:, :, None],
    )
    listing = jnp.any(naming, axis=1).astype(jnp.int32)
    earlier = jnp.cumsum(listing, axis=0) - listing
    placing = jnp.logical_and(
        listing.T[:, None, :] == 1,
        earlier.T[:, None, :] == jnp.arange(capacity, dtype=jnp.int32)[None, :, None],
    )
    placing = placing.astype(jnp.float32).reshape(owners * capacity, tiles_here)
    slot_rank = jnp.take_along_axis(earlier, block_list, axis=1)
    route_code = jnp.where(usable, block_list * capacity + slot_rank, -1)
    outgoing = jnp.dot(
        placing.astype(jnp.bfloat16),
        points.reshape(tiles_here, tile_rows * width),
        preferred_element_type=jnp.float32,
    )
    outgoing = outgoing.astype(jnp.bfloat16).reshape(owners, slot_rows, width)
    arrived = lax.all_to_all(outgoing, "cent", split_axis=0, concat_axis=0, tiled=True)
    incoming = arrived.reshape(owners * slot_rows, width)
    logits = (
        lax.dot_general(
            incoming,
            lax.all_gather(centroids, "dp", axis=1, tiled=True)[0],
            (((1,), (1,)), ((), ())),
            preferred_element_type=jnp.float32,
        )
        * scale
    )
    peaks = jnp.max(logits, axis=1)
    totals = jnp.sum(jnp.exp(logits - peaks[:, None]), axis=1)
    stats = jnp.stack([peaks.reshape(owners, slot_rows), totals.reshape(owners, slot_rows)], axis=1)
    back = lax.all_to_all(stats, "cent", split_axis=0, concat_axis=0, tiled=True)
    back_peaks = back[:, 0].reshape(owners * capacity, tile_rows)
    back_totals = back[:, 1].reshape(owners * capacity, tile_rows)
    lookup = jnp.where(usable, route_code, 0)
    tile_norms = combine_norms(back_peaks[lookup], back_totals[lookup], usable)
    empty = 1.0 - jnp.sum(placing, axis=1)
    slot_norms = (
        jnp.dot(placing, tile_norms, precision=lax.Precision.HIGHEST) + empty[:, None] * empty_norm
    )
    row_norms = lax.all_to_all(
        slot_norms.reshape(owners, slot_rows), "cent", split_axis=0, concat_axis=0, tiled=True
    ).reshape(-1)
    shares = jnp.exp(logits - row_norms[:, None]).astype(jnp.bfloat16)
    own_rows = centroids[0].astype(jnp.float32)
    marker = (jnp.arange(128, dtype=jnp.int32) == 0).astype(jnp.bfloat16)
    widened = jnp.concatenate(
        [incoming, jnp.broadcast_to(marker[None, :], (incoming.shape[0], 128))], axis=1
    )
    block_sums = lax.dot_general(
        shares, widened, (((0,), (0,)), ((), ())), preferred_element_type=jnp.float32
    )
    reduced = lax.psum_scatter(block_sums, "dp", scatter_dimension=0, tiled=True)
    new_sums = reduced[:, :width]
    new_mass = reduced[:, width]
    fresh = (new_sums + prior_weight * own_rows) / (new_mass[:, None] + prior_weight)
    return fresh[None]


def solution(mesh):
    in_specs = (
        P(("dp", "cent"), None),
        P(("dp", "cent"), None),
        P(("dp", "cent")),
        P("cent", "dp", None),
    )
    out_specs = P("cent", "dp", None)
    return jax.shard_map(
        per_device, mesh=mesh, in_specs=in_specs, out_specs=out_specs, check_vma=False
    )
```

profile of v0, /device:TPU:4, one launch (start us, length us, event | category | flops | bytes accessed | tf_op | source)
XLA Modules:
  0.0 250.5 jit_solution(18403319197507277494)
XLA Ops:
  6.5 0.7 all-gather.2.cloned.1.call-update
  7.3 0.7 iota_compare_fusion.1
  8.0 0.1 copy.33
  8.1 0.8 fusion.16
  9.1 1.3 reshape.116
  10.4 0.7 convolution_convert_fusion
  11.1 2.4 reshape.117
  13.4 9.5 %all-to-all-start = ((bf16[16,64,1024]{2,1,0:T(8,128)(2,1)}), bf16[16,64,1024]{2,1,0:T(8,128)(2,1)S(1)}, u32[]{:S(2)}, u32[]{:S(2)}) async-start(bf16[16,64,1024]{2,1,0:T(8,128)(2,1)} %reshape.117), calls=%async_computation | async-start | bytes 4194304 | tf_op jit(solution)/shard_map/all_to_all | solution.py:47
  23.3 0.7 gather_fusion.2
  24.3 0.1 fusion.11
  24.4 22.4 %all-to-all-done = bf16[16,64,1024]{2,1,0:T(8,128)(2,1)S(1)} async-done(((bf16[16,64,1024]{2,1,0:T(8,128)(2,1)}), bf16[16,64,1024]{2,1,0:T(8,128)(2,1)S(1)}, u32[]{:S(2)}, u32[]{:S(2)}) %all-to-all-start) | async-done | bytes 2097184 | tf_op jit(solution)/shard_map/all_to_all | solution.py:47
  46.8 39.0 %all-gather.2.cloned.1.call-done = bf16[1,1024,1024]{2,1,0:T(8,128)(2,1)} async-done(((bf16[1,32,1024]{2,1,0:T(8,128)(2,1)}), bf16[1,1024,1024]{2,1,0:T(8,128)(2,1)}) %all-gather.2.cloned.1.call-update) | async-done | bytes 2097168 | tf_op jit(solution)/shard_map/all_gather | solution.py:52
  85.8 6.0 %multiply_reduce_fusion = (f32[1024]{0:T(1024)S(1)}, f32[1024,1024]{0,1:T(8,128)}) fusion(bf16[1024,1024]{1,0:T(8,128)(2,1)S(1)} %bitcast.25, bf16[1,1024,1024]{2,1,0:T(8,128)(2,1)} %all-gather.2.cloned.1.call-done), kind=kOutput, calls=%fused_computation.6 | convolution fusion | flops 2149579776 | bytes 8392704 | tf_op jit(solution)/shard_map/dot_general | solution.py:50
  91.8 2.9 %exponential_reduce_fusion = f32[1024]{0:T(1024)S(1)} fusion(f32[1024,1024]{0,1:T(8,128)} %get-tuple-element.10, f32[1024]{0:T(1024)S(1)} %get-tuple-element.9), kind=kLoop, calls=%fused_computation.5 | loop fusion | flops 3144704 | bytes 4202496 | tf_op jit(solution)/shard_map/reduce_sum | solution.py:59
  94.8 0.7 reshape.173
  95.5 7.2 %all-to-all-start.1 = ((f32[16,1,128]{2,1,0:T(1,128)}), f32[16,1,128]{2,1,0:T(1,128)S(1)}, u32[]{:S(2)}, u32[]{:S(2)}) async-start(f32[16,1,128]{2,1,0:T(1,128)} %reshape.173), calls=%async_computation.1 | async-start | bytes 16384 | tf_op jit(solution)/shard_map/all_to_all | solution.py:61
  103.0 5.0 %all-to-all-done.1 = f32[16,1,128]{2,1,0:T(1,128)S(1)} async-done(((f32[16,1,128]{2,1,0:T(1,128)}), f32[16,1,128]{2,1,0:T(1,128)S(1)}, u32[]{:S(2)}, u32[]{:S(2)}) %all-to-all-start.1) | async-done | bytes 8224 | tf_op jit(solution)/shard_map/all_to_all | solution.py:61
  108.0 0.5 broadcast.144
  108.5 0.7 reduce.15
  109.4 0.6 gather_fusion.1
  110.1 0.6 gather_fusion
  110.7 0.1 select_reduce_fusion
  110.8 0.2 convolution_add_fusion
  111.0 0.7 all_to_all.14
  111.7 5.6 %all-to-all-start.2 = ((f32[16,1,64]{2,1,0:T(1,128)}), f32[16,1,64]{2,1,0:T(1,128)S(1)}, u32[]{:S(2)}, u32[]{:S(2)}) async-start(f32[16,1,64]{2,1,0:T(1,128)} %bitcast.7), calls=%async_computation.2 | async-start | bytes 16384 | tf_op jit(solution)/shard_map/all_to_all | solution.py:70
  117.4 5.2 %all-to-all-done.2 = f32[16,1,64]{2,1,0:T(1,128)S(1)} async-done(((f32[16,1,64]{2,1,0:T(1,128)}), f32[16,1,64]{2,1,0:T(1,128)S(1)}, u32[]{:S(2)}, u32[]{:S(2)}) %all-to-all-start.2) | async-done | bytes 4128 | tf_op jit(solution)/shard_map/all_to_all | solution.py:70
  122.6 0.5 broadcast.143
  123.1 0.7 reduce.14
  123.9 7.4 %fusion = f32[1024,1152]{1,0:T(8,128)} fusion(bf16[1024,1024]{1,0:T(8,128)(2,1)S(1)} %bitcast.26, f32[1024,1024]{0,1:T(8,128)} %get-tuple-element.10, f32[1024]{0:T(1024)S(1)} %sub.54, bf16[1152]{0:T(1024)(128)(2,1)S(1)} %pad.1.clone), kind=kOutput, calls=%fused_computation.7 | convolution fusion | flops 2423783424 | bytes 11016448 | tf_op jit(solution)/shard_map/dot_general | solution.py:79
  131.3 109.9 %reduce-scatter.2.cloned.1.call-done = f32[32,1152]{1,0:T(8,128)} async-done(((f32[1024,1152]{1,0:T(8,128)}), f32[32,1152]{1,0:T(8,128)}) %reduce-scatter.2.cloned.1.call-update) | async-done | bytes 147472 | tf_op jit(solution)/shard_map/reduce_scatter | solution.py:82
  241.2 0.8 fusion.10
  242.0 1.6 fusion.9
  (45 shorter events, 1.7 us)
Async XLA Ops:
  6.5 79.2 %all-gather.2.cloned.1.call-start = ((), (), s32[]{:S(2)}) async-start(), calls=%async_computation.4 | async-start | bytes 2162688 | tf_op jit(solution)/shard_map/all_gather | solution.py:52
  11.0 11.9 %copy-start.1 = (s32[8,3]{0,1:T(4,128)S(1)}, s32[8,3]{0,1:T(4,128)}, u32[]{:S(2)}) copy-start(s32[8,3]{0,1:T(4,128)} %param.5) | copy-start | bytes 292
  13.4 10.7 %copy-start.2 = (s32[8]{0:T(128)S(1)}, s32[8]{0:T(128)}, u32[]{:S(2)}) copy-start(s32[8]{0:T(128)} %param.6) | copy-start | bytes 100
  13.4 33.3 %all-to-all-start = ((bf16[16,64,1024]{2,1,0:T(8,128)(2,1)}), bf16[16,64,1024]{2,1,0:T(8,128)(2,1)S(1)}, u32[]{:S(2)}, u32[]{:S(2)}) async-start(bf16[16,64,1024]{2,1,0:T(8,128)(2,1)} %reshape.117), calls=%async_computation | async-start | bytes 4194304 | tf_op jit(solution)/shard_map/all_to_all | solution.py:47
  95.5 12.5 %all-to-all-start.1 = ((f32[16,1,128]{2,1,0:T(1,128)}), f32[16,1,128]{2,1,0:T(1,128)S(1)}, u32[]{:S(2)}, u32[]{:S(2)}) async-start(f32[16,1,128]{2,1,0:T(1,128)} %reshape.173), calls=%async_computation.1 | async-start | bytes 16384 | tf_op jit(solution)/shard_map/all_to_all | solution.py:61
  111.7 10.9 %all-to-all-start.2 = ((f32[16,1,64]{2,1,0:T(1,128)}), f32[16,1,64]{2,1,0:T(1,128)S(1)}, u32[]{:S(2)}, u32[]{:S(2)}) async-start(f32[16,1,64]{2,1,0:T(1,128)} %bitcast.7), calls=%async_computation.2 | async-start | bytes 16384 | tf_op jit(solution)/shard_map/all_to_all | solution.py:70
  117.3 123.8 %reduce-scatter.2.cloned.1.call-start = ((), (), s32[]{:S(2)}) async-start(), calls=%async_computation.5 | async-start | bytes 4866048 | tf_op jit(solution)/shard_map/reduce_scatter | solution.py:82
  131.3 110.7 %copy-start = (bf16[1,32,1024]{2,1,0:T(8,128)(2,1)S(1)}, bf16[1,32,1024]{2,1,0:T(8,128)(2,1)}, u32[]{:S(2)}) copy-start(bf16[1,32,1024]{2,1,0:T(8,128)(2,1)} %param.7) | copy-start | bytes 196612
Sparse Core Ops, SparseCore 0:
  9.5 76.2 all-gather.1
  131.4 109.7 reduce-scatter.1
where the time goes:
time: 251 us; the launch traced here: 250 us
  waiting for transfers between devices  182 us (73%)
  starting transfers between devices  22.4 us (9%)
  matrix products  14.2 us (6%)
  between operations  13.6 us (5%)
  local copies, waits for them, and re-layouts  9.44 us (4%)
  other arithmetic  8.68 us (3%)
    reduce_scatter x1, waiting for transfers between devices, per_device(): lax.psum_scatter(block_sums, 'dp', scatter_dimension=0, tiled=True)  110 us
    all_gather x1, waiting for transfers between devices, per_device(): lax.all_gather(centroids, 'dp', axis=1, tiled=True)[0]  39 us
    all_to_all x1, waiting for transfers between devices, per_device(): lax.all_to_all(outgoing, 'cent', split_axis=0, concat_axis=0, tiled=True)  22.4 us
    all_to_all x1, starting transfers between devices, per_device(): lax.all_to_all(outgoing, 'cent', split_axis=0, concat_axis=0, tiled=True)  9.52 us
    dot_general x1, matrix products, per_device(): lax.dot_general(shares, widened, (((0,), (0,)), ((), ())), preferred_elem...  7.39 us
    all_to_all x1, starting transfers between devices, per_device(): lax.all_to_all(stats, 'cent', split_axis=0, concat_axis=0, tiled=True)  7.25 us
    dot_general x1, matrix products, per_device(): lax.dot_general(incoming, lax.all_gather(centroids, 'dp', axis=1, tiled=T...  5.98 us
    all_to_all x1, starting transfers between devices, per_device(): lax.all_to_all(slot_norms.reshape(owners, slot_rows), 'cent', split_axis=...  5.6 us
  transfers between devices with their start and end apart: 5, of which 5 were waited for; matrix products, arithmetic and copies ran while one was open for 3% of the time, Pallas kernels for 0%

commit v1 on v0

--- a/solution.py
+++ b/solution.py
@@ -49,7 +49,9 @@
     logits = (
         lax.dot_general(
             incoming,
-            lax.all_gather(centroids, "dp", axis=1, tiled=True)[0],
+            jnp.concatenate(
+                lax.all_to_all(jnp.stack([centroids] * lax.axis_size("dp")), "dp", 0, 0), axis=1
+            )[0],
             (((1,), (1,)), ((), ())),
             preferred_element_type=jnp.float32,
         )

time: 251 us -> 323 us (1.29)
  the two profiles are of different devices: /device:TPU:4 before, /device:TPU:2 now
where the time goes in v1:
time: 323 us; the launch traced here: 322 us
  waiting for transfers between devices  215 us (67%)
  blocking collectives  34.7 us (11%)
  starting transfers between devices  25 us (8%)
  matrix products  14.2 us (4%)
  between operations  13.6 us (4%)
  local copies, waits for them, and re-layouts  11 us (3%)
  other arithmetic  8.68 us (3%)
    reduce_scatter x1, waiting for transfers between devices, per_device(): lax.psum_scatter(block_sums, 'dp', scatter_dimension=0, tiled=True)  105 us
    all_to_all x1, waiting for transfers between devices, per_device(): lax.all_to_all(jnp.stack([centroids] * lax.axis_size('dp')), 'dp', 0, 0)  97.7 us
    all_to_all x1, blocking collectives, per_device(): lax.all_to_all(outgoing, 'cent', split_axis=0, concat_axis=0, tiled=True)  34.7 us
    all_to_all x1, starting transfers between devices, per_device(): lax.all_to_all(jnp.stack([centroids] * lax.axis_size('dp')), 'dp', 0, 0)  15.6 us
    dot_general x1, matrix products, per_device(): lax.dot_general(shares, widened, (((0,), (0,)), ((), ())), preferred_elem...  7.39 us
  transfers between devices with their start and end apart: 4, of which 4 were waited for; matrix products, arithmetic and copies ran while one was open for 1% of the time, Pallas kernels for 0%

profile of v1, /device:TPU:2, one launch (start us, length us, event | category | flops | bytes accessed | tf_op | source)
XLA Modules:
  0.0 322.3 jit_solution(8725182225531531367)
XLA Ops:
  6.5 0.7 iota_compare_fusion.1
  7.3 0.1 copy.33
  7.4 0.8 fusion.14
  8.3 1.3 reshape.117
  9.6 0.7 convolution_convert_fusion
  10.3 2.4 reshape.118
  12.7 34.7 %all_to_all.24 = bf16[16,64,1024]{2,1,0:T(8,128)(2,1)S(1)} all-to-all(bf16[16,64,1024]{2,1,0:T(8,128)(2,1)} %reshape.118), channel_id=1, replica_groups=mesh['dp'=32,'cent'=16] {'cent'}, dimensions={0} | all-to-all | bytes 4194304 | tf_op jit(solution)/shard_map/all_to_all | solution.py:47
  47.4 1.6 stack.4
  48.9 15.6 %all-to-all-start.1 = ((bf16[32,1,32,1024]{3,2,1,0:T(8,128)(2,1)}), bf16[32,1,32,1024]{3,2,1,0:T(8,128)(2,1)}, u32[]{:S(2)}, u32[]{:S(2)}) async-start(bf16[32,1,32,1024]{3,2,1,0:T(8,128)(2,1)} %stack.4), calls=%async_computation.1 | async-start | bytes 4194304 | tf_op jit(solution)/shard_map/all_to_all | solution.py:53
  64.9 0.7 gather_fusion.2
  65.9 0.1 fusion.9
  66.0 97.7 %all-to-all-done.1 = bf16[32,1,32,1024]{3,2,1,0:T(8,128)(2,1)} async-done(((bf16[32,1,32,1024]{3,2,1,0:T(8,128)(2,1)}), bf16[32,1,32,1024]{3,2,1,0:T(8,128)(2,1)}, u32[]{:S(2)}, u32[]{:S(2)}) %all-to-all-start.1) | async-done | bytes 2097184 | tf_op jit(solution)/shard_map/all_to_all | solution.py:53
  163.7 6.0 %multiply_reduce_fusion = (f32[1024]{0:T(1024)S(1)}, f32[1024,1024]{0,1:T(8,128)}) fusion(bf16[1024,1024]{1,0:T(8,128)(2,1)S(1)} %bitcast.21, bf16[1024,1024]{1,0:T(8,128)(2,1)} %bitcast.5), kind=kOutput, calls=%fused_computation.6 | convolution fusion | flops 2149579776 | bytes 8392704 | tf_op jit(solution)/shard_map/dot_general | solution.py:50
  169.8 2.9 exponential_reduce_fusion
  172.8 0.7 reshape.173
  173.5 4.7 %all-to-all-start.2 = ((f32[16,1,128]{2,1,0:T(1,128)}), f32[16,1,128]{2,1,0:T(1,128)S(1)}, u32[]{:S(2)}, u32[]{:S(2)}) async-start(f32[16,1,128]{2,1,0:T(1,128)} %reshape.173), calls=%async_computation.2 | async-start | bytes 16384 | tf_op jit(solution)/shard_map/all_to_all | solution.py:63
  178.5 5.9 %all-to-all-done.2 = f32[16,1,128]{2,1,0:T(1,128)S(1)} async-done(((f32[16,1,128]{2,1,0:T(1,128)}), f32[16,1,128]{2,1,0:T(1,128)S(1)}, u32[]{:S(2)}, u32[]{:S(2)}) %all-to-all-start.2) | async-done | bytes 8224 | tf_op jit(solution)/shard_map/all_to_all | solution.py:63
  184.4 0.5 broadcast.147
  184.9 0.7 reduce.15
  185.8 0.6 gather_fusion.1
  186.4 0.6 gather_fusion
  187.1 0.1 select_reduce_fusion
  187.2 0.2 convolution_add_fusion
  187.4 0.7 all_to_all.18
  188.1 4.7 %all-to-all-start.3 = ((f32[16,1,64]{2,1,0:T(1,128)}), f32[16,1,64]{2,1,0:T(1,128)S(1)}, u32[]{:S(2)}, u32[]{:S(2)}) async-start(f32[16,1,64]{2,1,0:T(1,128)} %bitcast.8), calls=%async_computation.3 | async-start | bytes 16384 | tf_op jit(solution)/shard_map/all_to_all | solution.py:72
  192.9 6.1 %all-to-all-done.3 = f32[16,1,64]{2,1,0:T(1,128)S(1)} async-done(((f32[16,1,64]{2,1,0:T(1,128)}), f32[16,1,64]{2,1,0:T(1,128)S(1)}, u32[]{:S(2)}, u32[]{:S(2)}) %all-to-all-start.3) | async-done | bytes 4128 | tf_op jit(solution)/shard_map/all_to_all | solution.py:72
  199.0 0.5 broadcast.146
  199.5 0.7 reduce.14
  200.3 7.4 %fusion = f32[1024,1152]{1,0:T(8,128)} fusion(bf16[1024,1024]{1,0:T(8,128)(2,1)S(1)} %bitcast.22, f32[1024,1024]{0,1:T(8,128)} %get-tuple-element.10, f32[1024]{0:T(1024)S(1)} %sub.54, bf16[1152]{0:T(1024)(128)(2,1)S(1)} %pad.1.clone), kind=kOutput, calls=%fused_computation.7 | convolution fusion | flops 2423783424 | bytes 11016448 | tf_op jit(solution)/shard_map/dot_general | solution.py:81
  207.7 105.4 %reduce-scatter.2.cloned.1.call-done = f32[32,1152]{1,0:T(8,128)} async-done(((f32[1024,1152]{1,0:T(8,128)}), f32[32,1152]{1,0:T(8,128)}) %reduce-scatter.2.cloned.1.call-update) | async-done | bytes 147472 | tf_op jit(solution)/shard_map/reduce_scatter | solution.py:84
  313.0 0.8 fusion.8
  313.9 1.6 fusion.7
  (44 shorter events, 1.7 us)
Async XLA Ops:
  10.3 37.1 %copy-start = (bf16[1,32,1024]{2,1,0:T(8,128)(2,1)S(1)}, bf16[1,32,1024]{2,1,0:T(8,128)(2,1)}, u32[]{:S(2)}) copy-start(bf16[1,32,1024]{2,1,0:T(8,128)(2,1)} %param.7) | copy-start | bytes 196612
  47.4 17.1 %copy-start.1 = (s32[8,3]{0,1:T(4,128)S(1)}, s32[8,3]{0,1:T(4,128)}, u32[]{:S(2)}) copy-start(s32[8,3]{0,1:T(4,128)} %param.5) | copy-start | bytes 292
  48.9 16.8 %copy-start.2 = (s32[8]{0:T(128)S(1)}, s32[8]{0:T(128)}, u32[]{:S(2)}) copy-start(s32[8]{0:T(128)} %param.6) | copy-start | bytes 100
  48.9 114.8 %all-to-all-start.1 = ((bf16[32,1,32,1024]{3,2,1,0:T(8,128)(2,1)}), bf16[32,1,32,1024]{3,2,1,0:T(8,128)(2,1)}, u32[]{:S(2)}, u32[]{:S(2)}) async-start(bf16[32,1,32,1024]{3,2,1,0:T(8,128)(2,1)} %stack.4), calls=%async_computation.1 | async-start | bytes 4194304 | tf_op jit(solution)/shard_map/all_to_all | solution.py:53
  173.5 10.9 %all-to-all-start.2 = ((f32[16,1,128]{2,1,0:T(1,128)}), f32[16,1,128]{2,1,0:T(1,128)S(1)}, u32[]{:S(2)}, u32[]{:S(2)}) async-start(f32[16,1,128]{2,1,0:T(1,128)} %reshape.173), calls=%async_computation.2 | async-start | bytes 16384 | tf_op jit(solution)/shard_map/all_to_all | solution.py:63
  188.1 10.9 %all-to-all-start.3 = ((f32[16,1,64]{2,1,0:T(1,128)}), f32[16,1,64]{2,1,0:T(1,128)S(1)}, u32[]{:S(2)}, u32[]{:S(2)}) async-start(f32[16,1,64]{2,1,0:T(1,128)} %bitcast.8), calls=%async_computation.3 | async-start | bytes 16384 | tf_op jit(solution)/shard_map/all_to_all | solution.py:72
  192.8 120.2 %reduce-scatter.2.cloned.1.call-start = ((), (), s32[]{:S(2)}) async-start(), calls=%async_computation.5 | async-start | bytes 4866048 | tf_op jit(solution)/shard_map/reduce_scatter | solution.py:84
Sparse Core Ops, SparseCore 0:
  207.8 105.1 reduce-scatter.1
